TPU v7x, 256 devices: a whole 4x4x8 slice. The times are simulated.
256 devices in a mesh: req: 32 (over y, x, core), tp: 8 (over z).
Axes of the slice: x: 4, y: 4, z: 8, core: 2. Of those that a mesh axis runs over, the one named last changes fastest.
Arguments:
- tokens: bfloat16 [256, 4, 1536], P('req'), may hold values from -6 to 6
- lengths: int32 [256], P('req'), may hold values from 16 to 32768, as said below
- page_table: int32 [256, 9], P('req'), may hold values from 0 to 2303, as said below
- kv_pages: bfloat16 [2304, 2, 128, 128], P('req'), may hold values from -480 to 480
- norm_gain: float32 [1536], replicated, may hold values from 0.1 to 1.9
- query_weight: bfloat16 [1536, 1024], P(None, 'tp'), may hold values from -0.15625 to 0.15625
- key_weight: bfloat16 [1536, 128], replicated, may hold values from -0.15625 to 0.15625
- value_weight: bfloat16 [1536, 128], replicated, may hold values from -0.15625 to 0.15625
- out_weight: bfloat16 [1024, 1536], P('tp'), may hold values from -0.1875 to 0.1875
- mlp_gain: float32 [1536], replicated, may hold values from 0.1 to 1.9
- gate_weight: bfloat16 [1536, 4608], P(None, 'tp'), may hold values from -0.15625 to 0.15625
- up_weight: bfloat16 [1536, 4608], P(None, 'tp'), may hold values from -0.15625 to 0.15625
- down_weight: bfloat16 [4608, 1536], P('tp'), may hold values from -0.09375 to 0.09375
Outputs:
- layer_out: bfloat16 [256, 4, 1536], P('req')
Inputs may be any that keep to these rules, and one draw needn't show every extreme that they name: `lengths`: one request has exactly 32768 cached positions in every draw. `page_table`: all entries together are a permutation of the 2304 pool pages. Entry (r, j) is pool page r * 9 + j, in the part of the pool held with request r, except for spilled entries chosen from the seed (about a fifth of all); the spilled entries hold one another's pool pages in an order drawn from the seed, mostly on other devices of req.
All inputs are finite; a program needn't handle non-finite values.
Results may differ from a plain program's by a relative error of at most 0.0095.
The roundings to bfloat16 on the way count: a program that leaves them out, or rounds other values in their place, can miss the bound.
Values may be sent and summed in bfloat16 or wider, within the bound.
No kernel may reach another device: no remote copies, remote signals or barrier semaphores. Data moves between devices by JAX's collectives and lax.ppermute only.
A program may use at most 128 MiB of HBM per device.

v0:
```python
import jax
import jax.numpy as jnp
from jax import lax
from jax.sharding import PartitionSpec as P

WINDOW = 1024
negative = -1e30
epsilon = 1e-06


def rms_norm(values, gain):
    return values * lax.rsqrt(jnp.mean(values * values, axis=-1, keepdims=True) + epsilon) * gain


def body(
    tokens,
    lengths,
    page_table,
    kv_pages,
    norm_gain,
    query_weight,
    key_weight,
    value_weight,
    out_weight,
    mlp_gain,
    gate_weight,
    up_weight,
    down_weight,
):
    req_dev, steps, width = tokens.shape
    head_dim = key_weight.shape[1]
    heads_dev = query_weight.shape[1] // head_dim
    pool_size = kv_pages.shape[0]
    page_size = kv_pages.shape[2]
    window_pages = page_table.shape[1]
    token_rows = tokens.reshape(req_dev * steps, width)
    normed = rms_norm(token_rows.astype(jnp.float32), norm_gain).astype(jnp.bfloat16)
    queries = (
        jnp.dot(normed, query_weight, preferred_element_type=jnp.float32) * head_dim ** (-0.5)
    ).astype(jnp.bfloat16)
    key_new = jnp.dot(normed, key_weight, preferred_element_type=jnp.float32).astype(jnp.bfloat16)
    value_new = jnp.dot(normed, value_weight, preferred_element_type=jnp.float32).astype(
        jnp.bfloat16
    )
    all_lengths, all_table = (
        lax.all_gather(lengths, "req", axis=0, tiled=True),
        lax.all_gather(page_table, "req", axis=0, tiled=True),
    )
    all_queries = lax.all_gather(
        queries.reshape(req_dev, steps, heads_dev * head_dim), "req", axis=0, tiled=True
    )
    requests = all_lengths.shape[0]
    flat_table = all_table.reshape(-1)
    local_slot = flat_table - lax.axis_index("req") * pool_size
    inside = (local_slot >= 0) & (local_slot < pool_size)
    owner_entry = (
        jnp.zeros((pool_size,), jnp.int32)
        .at[jnp.where(inside, local_slot, pool_size)]
        .set(jnp.arange(flat_table.shape[0], dtype=jnp.int32), mode="drop")
    )
    page_request = owner_entry // window_pages
    page_number = owner_entry % window_pages
    page_length = all_lengths[page_request]
    first_page = jnp.maximum(page_length - (WINDOW - 1), 0) // page_size
    position = (first_page + page_number)[:, None] * page_size + jnp.arange(
        page_size, dtype=jnp.int32
    )[None, :]
    current = page_length[:, None] + jnp.arange(steps, dtype=jnp.int32)[None, :]
    visible = (position[:, None, :] < page_length[:, None, None]) & (
        position[:, None, :] > current[:, :, None] - WINDOW
    )
    visible = visible[:, :, None, :]
    page_queries = all_queries[page_request]
    scores = jnp.einsum(
        "pqd,pkd->pqk", page_queries, kv_pages[:, 0], preferred_element_type=jnp.float32
    )
    scores = jnp.where(visible, scores.reshape(pool_size, steps, heads_dev, page_size), negative)
    block_max = jnp.max(scores, axis=-1)
    weights = jnp.where(visible, jnp.exp(scores - block_max[..., None]), 0.0)
    block_total = jnp.sum(weights, axis=-1)
    block_out = jnp.einsum(
        "pqk,pkd->pqd",
        weights.astype(jnp.bfloat16).reshape(pool_size, steps * heads_dev, page_size),
        kv_pages[:, 1],
        preferred_element_type=jnp.float32,
    )
    block_out = block_out.reshape(pool_size, steps, heads_dev, head_dim)
    request_max = jnp.maximum(
        jax.ops.segment_max(block_max, page_request, num_segments=requests), negative
    )
    start_row = lax.axis_index("req") * req_dev
    cache_max = lax.pmax(request_max, "req")
    scale = jnp.exp(block_max - cache_max[page_request])
    sent_out = jax.ops.segment_sum(
        block_out * scale[..., None], page_request, num_segments=requests
    )
    sent_total = jax.ops.segment_sum(block_total * scale, page_request, num_segments=requests)
    cache_out, cache_total = (
        lax.psum_scatter(sent_out, "req", scatter_dimension=0, tiled=True),
        lax.psum_scatter(sent_total, "req", scatter_dimension=0, tiled=True),
    )
    mine_max = lax.dynamic_slice_in_dim(cache_max, start_row, req_dev, 0)
    local_queries = queries.reshape(req_dev, steps, heads_dev, head_dim)
    new_scores = jnp.einsum(
        "rshd,rtd->rsht",
        local_queries,
        key_new.reshape(req_dev, steps, head_dim),
        preferred_element_type=jnp.float32,
    )
    causal = (jnp.arange(steps)[None, :] <= jnp.arange(steps)[:, None])[None, :, None, :]
    new_scores = jnp.where(causal, new_scores, negative)
    new_max = jnp.max(new_scores, axis=-1)
    new_weights = jnp.where(causal, jnp.exp(new_scores - new_max[..., None]), 0.0)
    new_total = jnp.sum(new_weights, axis=-1)
    new_out = jnp.einsum(
        "rsht,rtd->rshd",
        new_weights.astype(jnp.bfloat16),
        value_new.reshape(req_dev, steps, head_dim),
        preferred_element_type=jnp.float32,
    )
    overall = jnp.maximum(mine_max, new_max)
    cache_scale = jnp.exp(mine_max - overall)
    new_scale = jnp.exp(new_max - overall)
    total = cache_total * cache_scale + new_total * new_scale
    summed = cache_out * cache_scale[..., None] + new_out * new_scale[..., None]
    attended = (
        (summed / total[..., None])
        .astype(jnp.bfloat16)
        .reshape(req_dev * steps, heads_dev * head_dim)
    )
    projected = jnp.dot(attended, out_weight, preferred_element_type=jnp.float32)
    attn_total = lax.psum(projected, "tp")
    residual = (token_rows.astype(jnp.float32) + attn_total).astype(jnp.bfloat16)
    mlp_in = rms_norm(residual.astype(jnp.float32), mlp_gain).astype(jnp.bfloat16)
    gate = jnp.dot(mlp_in, gate_weight, preferred_element_type=jnp.float32)
    upward = jnp.dot(mlp_in, up_weight, preferred_element_type=jnp.float32)
    hidden = (jax.nn.gelu(gate, approximate=True) * upward).astype(jnp.bfloat16)
    mlp_total = lax.psum(
        jnp.dot(hidden, down_weight, preferred_element_type=jnp.float32).astype(jnp.bfloat16), "tp"
    ).astype(jnp.float32)
    layer_out = (residual.astype(jnp.float32) + mlp_total).astype(jnp.bfloat16)
    return layer_out.reshape(req_dev, steps, width)


def solution(mesh):
    return jax.shard_map(
        body,
        mesh=mesh,
        in_specs=(
            P("req", None, None),
            P("req"),
            P("req", None),
            P("req", None, None, None),
            P(),
            P(None, "tp"),
            P(),
            P(),
            P("tp", None),
            P(),
            P(None, "tp"),
            P(None, "tp"),
            P("tp", None),
        ),
        out_specs=P("req", None, None),
        check_vma=False,
    )
```

profile of v0, /device:TPU:2, one launch (start us, length us, event | category | flops | bytes accessed | tf_op | source)
XLA Modules:
  0.0 512.9 jit_solution(16299514413610461038)
XLA Ops:
  6.5 0.0 copy-start
  6.5 0.0 reduce-scatter.6.cloned.1.call-start
  6.5 1.4 fusion.63
  8.6 0.9 dynamic-update-slice
  9.5 15.7 %all-reduce = s32[256]{0:T(256)S(1)} all-reduce(s32[256]{0:T(256)S(1)} %dynamic-update-slice), channel_id=1, replica_groups=mesh['req'=32,'tp'=8] {'req'}, use_global_device_ids=true, to_apply=%add | all-reduce | flops 256 | bytes 2048
  25.2 23.4 %all_gather.9 = s32[256,9]{1,0:T(8,128)S(1)} all-gather(s32[8,9]{1,0:T(8,128)} %param.15), channel_id=1, replica_groups=mesh['req'=32,'tp'=8] {'req'}, dimensions={0}, use_global_device_ids=true | all-gather | bytes 9504 | tf_op jit(solution)/shard_map/all_gather | solution.py:47
  48.5 0.2 sub.78
  48.8 9.0 %scatter_custom_fusion = s32[72]{0:T(128)S(1)} fusion(s32[2304]{0:T(1024)S(1)} %fusion.44, s32[2304]{0:T(1024)S(1)} %iota.34, s32[]{:T(128)} %constant.27.clone.1), kind=kCustom, calls=%fused_computation.93 | custom fusion | bytes 292 | tf_op jit(solution)/shard_map/scatter | solution.py:59
  57.8 1.3 gather_fusion
  59.1 0.1 broadcast_compare_fusion
  59.2 0.0 copy-start.8
  59.2 0.1 iota_add_fusion
  59.3 0.1 add_add_fusion
  59.4 1.0 multiply_reduce_fusion
  60.4 0.9 reshape.246
  61.4 0.1 rsqrt.20
  61.4 0.8 multiply_convert_fusion
  62.2 0.0 copy-done.2
  62.2 0.2 fusion.14
  62.4 22.6 %all_gather.11 = bf16[256,4,128]{2,1,0:T(4,128)(2,1)S(1)} all-gather(bf16[8,4,128]{2,1,0:T(4,128)(2,1)S(1)} %bitcast.89), channel_id=1, replica_groups=mesh['req'=32,'tp'=8] {'req'}, dimensions={0}, use_global_device_ids=true | all-gather | bytes 270336 | tf_op jit(solution)/shard_map/all_gather | solution.py:49
  85.0 0.7 gather_fusion.1
  85.7 3.1 fusion.64
  88.8 1.0 scatter_custom_fusion.1
  89.8 123.3 %pmax.7 = f32[256,4,1]{1,0,2:T(8,128)S(1)} all-reduce(f32[256,4,1]{1,0,2:T(8,128)S(1)} %maximum_bitcast_fusion), channel_id=1, replica_groups=mesh['req'=32,'tp'=8] {'req'}, use_global_device_ids=true, to_apply=%region_4.5 | all-reduce | flops 1024 | bytes 8192 | tf_op jit(solution)/shard_map/pmax | solution.py:92
  213.1 0.6 gather_fusion.2
  213.7 0.0 copy-start.6
  213.8 0.0 copy-done.8
  213.8 0.0 copy-done.4
  213.8 2.5 fusion.9
  216.3 0.1 broadcast.190
  216.3 0.0 copy-done.6
  216.3 3.5 scatter_fusion
  219.8 0.0 copy-start.1
  219.8 0.8 copy.86
  220.7 0.0 reduce-scatter.6.cloned.1.call-update
  220.7 0.0 copy-start.9
  220.7 0.0 all-reduce.5.cloned.1.call-start
  220.8 0.0 copy-done.3
  220.8 0.2 convolution_convert_fusion.2
  221.0 0.1 fusion.65
  221.1 0.1 copy.56
  221.2 0.1 select_reduce_fusion
  221.3 0.1 copy.59
  221.4 0.1 fusion.45
  221.5 0.1 copy.81
  221.6 0.1 copy.63
  221.7 1.3 fusion.57
  222.9 1.2 scatter_custom_fusion.3
  224.7 123.8 %all-reduce.1 = f32[256,4,1]{1,0,2:T(8,128)S(1)} all-reduce(f32[256,4,1]{1,0,2:T(8,128)S(1)} %bitcast.88), channel_id=3, replica_groups=mesh['req'=32,'tp'=8] {'req'}, use_global_device_ids=true, to_apply=%region_10.11.clone | all-reduce | flops 1024 | bytes 8192
  348.6 1.2 convolution_convert_fusion.1
  349.8 0.0 reduce-scatter.6.cloned.1.call-done
  349.8 0.7 reshape.332
  350.5 0.1 fusion.17
  350.7 0.9 fusion.66
  351.5 0.0 all-reduce.5.cloned.1.call-update
  351.6 0.0 all-reduce.7.cloned.1.call-start
  351.6 75.7 %all-reduce.5.cloned.1.call-done = f32[32,1536]{1,0:T(8,128)} async-done(((f32[32,1536]{1,0:T(8,128)}), f32[32,1536]{1,0:T(8,128)}) %all-reduce.5.cloned.1.call-update) | async-done | bytes 196624 | tf_op jit(solution)/shard_map/psum | solution.py:132
  427.3 1.1 fusion.18
  428.4 2.1 fusion.42
  430.5 3.2 convolution_convert_fusion
  433.7 0.0 all-reduce.7.cloned.1.call-update
  433.7 71.0 %all-reduce.7.cloned.1.call-done = bf16[32,1536]{1,0:T(8,128)(2,1)} async-done(((bf16[32,1536]{1,0:T(8,128)(2,1)}), bf16[32,1536]{1,0:T(8,128)(2,1)}) %all-reduce.7.cloned.1.call-update) | async-done | bytes 98320 | tf_op jit(solution)/shard_map/psum | solution.py:138
  504.8 0.9 fusion.21
  505.7 0.7 reshape.245
  (23 shorter events, 0.2 us)
Async XLA Ops:
  6.5 424.0 %copy-start = (bf16[576,1536]{1,0:T(8,128)(2,1)S(1)}, bf16[576,1536]{1,0:T(8,128)(2,1)}, u32[]{:S(2)}) copy-start(bf16[576,1536]{1,0:T(8,128)(2,1)} %param.25) | copy-start | bytes 5308420
  6.5 55.7 %copy-start.2 = (bf16[1536,128]{1,0:T(8,128)(2,1)S(1)}, bf16[1536,128]{1,0:T(8,128)(2,1)}, u32[]{:S(2)}) copy-start(bf16[1536,128]{1,0:T(8,128)(2,1)} %param.18) | copy-start | bytes 1179652
  6.5 343.3 %reduce-scatter.6.cloned.1.call-start = ((), (), s32[]{:S(2)}) async-start(), calls=%async_computation.3 | async-start | bytes 540672
  59.2 154.5 %copy-start.8 = (pred[72,128]{1,0:T(8,128)(4,1)}, pred[72,128]{1,0:T(8,128)(4,1)S(1)}, u32[]{:S(2)}) copy-start(pred[72,128]{1,0:T(8,128)(4,1)S(1)} %broadcast_compare_fusion) | copy-start | bytes 27652
  59.3 154.5 %copy-start.4 = (s32[72,128]{1,0:T(8,128)}, s32[72,128]{1,0:T(8,128)S(1)}, u32[]{:S(2)}) copy-start(s32[72,128]{1,0:T(8,128)S(1)} %iota_add_fusion) | copy-start | bytes 110596
  59.4 154.4 %copy-start.5 = (s32[72,4]{1,0:T(8,128)}, s32[72,4]{1,0:T(8,128)S(1)}, u32[]{:S(2)}) copy-start(s32[72,4]{1,0:T(8,128)S(1)} %add_add_fusion) | copy-start | bytes 3460
  88.8 125.0 %copy-start.7 = (f32[72,4,128]{2,1,0:T(4,128)}, f32[72,4,128]{2,1,0:T(4,128)S(1)}, u32[]{:S(2)}) copy-start(f32[72,4,128]{2,1,0:T(4,128)S(1)} %get-tuple-element.17) | copy-start | bytes 442372
  213.7 2.6 copy-start.6
  216.3 4.5 copy-start.3
  219.8 130.8 %copy-start.1 = (bf16[128,1536]{1,0:T(8,128)(2,1)S(1)}, bf16[128,1536]{1,0:T(8,128)(2,1)}, u32[]{:S(2)}) copy-start(bf16[128,1536]{1,0:T(8,128)(2,1)} %param.21) | copy-start | bytes 1179652
  220.7 207.7 %copy-start.9 = (f32[1536]{0:T(1024)S(1)}, f32[1536]{0:T(1024)}, u32[]{:S(2)}) copy-start(f32[1536]{0:T(1024)} %param.22) | copy-start | bytes 18436
  220.7 206.6 %all-reduce.5.cloned.1.call-start = ((), (), s32[]{:S(2)}) async-start(), calls=%async_computation.1 | async-start | bytes 393216 | tf_op jit(solution)/shard_map/psum | solution.py:132
  351.6 153.2 %all-reduce.7.cloned.1.call-start = ((), (), s32[]{:S(2)}) async-start(), calls=%async_computation.2 | async-start | bytes 196608 | tf_op jit(solution)/shard_map/psum | solution.py:138
Sparse Core Ops, SparseCore 0:
  220.8 87.7 reduce-scatter.5
  351.7 75.5 all-reduce.4
  433.8 70.8 all-reduce.6
where the time goes:
time: 514 us; the launch traced here: 513 us
  blocking collectives  309 us (60%)
  waiting for transfers between devices  147 us (29%)
  local copies, waits for them, and re-layouts  17.7 us (3%)
  between operations  14.6 us (3%)
  matrix products  13.5 us (3%)
  other arithmetic  11.4 us (2%)
    unnamed x2, blocking collectives  140 us
    pmax x1, blocking collectives, body(): cache_max = lax.pmax(request_max, 'req')  123 us
    psum x1, waiting for transfers between devices, body(): attn_total = lax.psum(projected, 'tp')  75.7 us
    psum x1, waiting for transfers between devices, body(): lax.psum(jnp.dot(hidden, down_weight, preferred_element_type=jnp.float32)...  71 us
    all_gather x1, blocking collectives, body(): lax.all_gather(page_table, 'req', axis=0, tiled=True)  23.4 us
    all_gather x1, blocking collectives, body(): lax.all_gather(queries.reshape(req_dev, steps, heads_dev * head_dim), 're...  22.6 us
  transfers between devices with their start and end apart: 3, of which 2 were waited for; matrix products, arithmetic and copies ran while one was open for 1% of the time, Pallas kernels for 0%

commit v1 on v0

--- a/solution.py
+++ b/solution.py
@@ -135,8 +135,12 @@
     gate = jnp.dot(mlp_in, gate_weight, preferred_element_type=jnp.float32)
     upward = jnp.dot(mlp_in, up_weight, preferred_element_type=jnp.float32)
     hidden = (jax.nn.gelu(gate, approximate=True) * upward).astype(jnp.bfloat16)
-    mlp_total = lax.psum(
-        jnp.dot(hidden, down_weight, preferred_element_type=jnp.float32).astype(jnp.bfloat16), "tp"
+    mlp_total = jnp.sum(
+        lax.all_gather(
+            jnp.dot(hidden, down_weight, preferred_element_type=jnp.float32).astype(jnp.bfloat16),
+            "tp",
+        ),
+        axis=0,
     ).astype(jnp.float32)
     layer_out = (residual.astype(jnp.float32) + mlp_total).astype(jnp.bfloat16)
     return layer_out.reshape(req_dev, steps, width)

time: 514 us -> 469 us (0.912)
  waiting for transfers between devices: 147 us -> 75.9 us
  blocking collectives: 309 us -> 335 us
    psum x1 -> x0, waiting for transfers between devices: 71 us -> none  [body(): lax.psum(jnp.dot(hidden, down_weight, preferred_element_type=jnp.float32)...]
    all_gather x0 -> x1, blocking collectives: none -> 26.5 us  [body(): lax.all_gather(jnp.dot(hidden, down_weight, preferred_element_type=jnp.fl...]
  transfers between devices with their start and end apart: 3 -> 2, of which waited for: 2 -> 1; matrix products, arithmetic and copies ran while one was open for 1% -> 1% of each run, Pallas kernels for 0% -> 0%
where the time goes in v1:
time: 469 us
  blocking collectives  335 us (71%)
  waiting for transfers between devices  75.9 us (16%)
  local copies, waits for them, and re-layouts  18.3 us (4%)
  between operations  15 us (3%)
  matrix products  13.6 us (3%)
  other arithmetic  10.6 us (2%)
    unnamed x2, blocking collectives  139 us
    pmax x1, blocking collectives, body(): cache_max = lax.pmax(request_max, 'req')  123 us
    psum x1, waiting for transfers between devices, body(): attn_total = lax.psum(projected, 'tp')  75.8 us
    all_gather x1, blocking collectives, body(): lax.all_gather(jnp.dot(hidden, down_weight, preferred_element_type=jnp.fl...  26.5 us
    all_gather x1, blocking collectives, body(): lax.all_gather(page_table, 'req', axis=0, tiled=True)  23.4 us
    all_gather x1, blocking collectives, body(): lax.all_gather(queries.reshape(req_dev, steps, heads_dev * head_dim), 're...  22.6 us
  transfers between devices with their start and end apart: 2, of which 1 were waited for; matrix products, arithmetic and copies ran while one was open for 1% of the time, Pallas kernels for 0%

profile of v1, /device:TPU:2, one launch (start us, length us, event | category | flops | bytes accessed | tf_op | source)
XLA Modules:
  0.0 468.6 jit_solution(1292504064180353443)
XLA Ops:
  6.5 0.0 copy-start
  6.5 0.0 reduce-scatter.6.cloned.1.call-start
  6.5 1.4 fusion.63
  8.6 0.9 dynamic-update-slice
  9.5 15.7 %all-reduce = s32[256]{0:T(256)S(1)} all-reduce(s32[256]{0:T(256)S(1)} %dynamic-update-slice), channel_id=1, replica_groups=mesh['req'=32,'tp'=8] {'req'}, use_global_device_ids=true, to_apply=%add | all-reduce | flops 256 | bytes 2048
  25.2 23.4 %all_gather.15 = s32[256,9]{1,0:T(8,128)S(1)} all-gather(s32[8,9]{1,0:T(8,128)} %param.15), channel_id=1, replica_groups=mesh['req'=32,'tp'=8] {'req'}, dimensions={0}, use_global_device_ids=true | all-gather | bytes 9504 | tf_op jit(solution)/shard_map/all_gather | solution.py:47
  48.5 0.2 sub.78
  48.8 9.0 %scatter_custom_fusion = s32[72]{0:T(128)S(1)} fusion(s32[2304]{0:T(1024)S(1)} %fusion.44, s32[2304]{0:T(1024)S(1)} %iota.34, s32[]{:T(128)} %constant.28.clone.1), kind=kCustom, calls=%fused_computation.93 | custom fusion | bytes 292 | tf_op jit(solution)/shard_map/scatter | solution.py:59
  57.8 1.3 gather_fusion
  59.1 0.1 broadcast_compare_fusion
  59.2 0.0 copy-start.11
  59.2 0.1 iota_add_fusion
  59.3 0.1 add_add_fusion
  59.4 1.0 multiply_reduce_fusion
  60.4 0.9 reshape.246
  61.4 0.1 rsqrt.20
  61.4 0.8 multiply_convert_fusion
  62.2 0.0 copy-done.5
  62.2 0.2 fusion.14
  62.4 22.6 %all_gather.17 = bf16[256,4,128]{2,1,0:T(4,128)(2,1)S(1)} all-gather(bf16[8,4,128]{2,1,0:T(4,128)(2,1)S(1)} %bitcast.91), channel_id=1, replica_groups=mesh['req'=32,'tp'=8] {'req'}, dimensions={0}, use_global_device_ids=true | all-gather | bytes 270336 | tf_op jit(solution)/shard_map/all_gather | solution.py:49
  85.0 0.7 gather_fusion.1
  85.7 3.1 fusion.64
  88.8 1.0 scatter_custom_fusion.1
  89.8 123.3 %pmax.7 = f32[256,4,1]{1,0,2:T(8,128)S(1)} all-reduce(f32[256,4,1]{1,0,2:T(8,128)S(1)} %maximum_bitcast_fusion), channel_id=1, replica_groups=mesh['req'=32,'tp'=8] {'req'}, use_global_device_ids=true, to_apply=%region_4.5 | all-reduce | flops 1024 | bytes 8192 | tf_op jit(solution)/shard_map/pmax | solution.py:92
  213.1 0.6 gather_fusion.2
  213.7 0.0 copy-start.9
  213.8 0.0 copy-done.11
  213.8 0.0 copy-done.7
  213.8 0.0 copy-done.8
  213.8 2.5 fusion.9
  216.3 0.1 broadcast.190
  216.3 0.0 copy-done.9
  216.3 3.5 scatter_fusion
  219.8 0.0 copy-start.4
  219.8 0.8 copy.86
  220.7 0.0 reduce-scatter.6.cloned.1.call-update
  220.7 0.0 all-reduce.4.cloned.1.call-start
  220.8 0.2 convolution_convert_fusion.2
  220.9 0.1 fusion.65
  221.1 0.1 copy.56
  221.2 0.1 select_reduce_fusion
  221.3 0.1 copy.59
  221.4 0.1 fusion.45
  221.5 0.1 copy.81
  221.5 0.1 copy.63
  221.7 1.3 fusion.57
  222.9 1.2 scatter_custom_fusion.3
  224.7 123.8 %all-reduce.1 = f32[256,4,1]{1,0,2:T(8,128)S(1)} all-reduce(f32[256,4,1]{1,0,2:T(8,128)S(1)} %bitcast.90), channel_id=4, replica_groups=mesh['req'=32,'tp'=8] {'req'}, use_global_device_ids=true, to_apply=%region_10.11.clone | all-reduce | flops 1024 | bytes 8192
  348.6 1.2 convolution_convert_fusion.1
  349.8 0.0 copy-start.12
  349.8 0.0 reduce-scatter.6.cloned.1.call-done
  349.8 0.7 reshape.333
  350.5 0.1 fusion.17
  350.7 0.9 fusion.66
  351.5 0.0 all-reduce.4.cloned.1.call-update
  351.6 75.8 %all-reduce.4.cloned.1.call-done = f32[32,1536]{1,0:T(8,128)} async-done(((f32[32,1536]{1,0:T(8,128)}), f32[32,1536]{1,0:T(8,128)}) %all-reduce.4.cloned.1.call-update) | async-done | bytes 196624 | tf_op jit(solution)/shard_map/psum | solution.py:132
  427.4 1.1 fusion.18
  428.5 0.0 copy-start.1
  428.5 0.6 copy-done.2
  429.1 2.8 fusion.42
  431.9 2.6 convolution_convert_fusion
  434.5 26.5 %all-gather = bf16[256,1536]{1,0:T(8,128)(2,1)S(1)} all-gather(bf16[32,1536]{1,0:T(8,128)(2,1)} %convolution_convert_fusion), channel_id=2, replica_groups=mesh['req'=32,'tp'=8] {'tp'}, dimensions={0}, use_global_device_ids=true | all-gather | bytes 884736 | tf_op jit(solution)/shard_map/all_gather | solution.py:139
  460.9 0.1 reduce_sum.58
  461.1 0.7 reshape.245
  (28 shorter events, 0.2 us)
Async XLA Ops:
  6.5 425.3 %copy-start = (bf16[576,1536]{1,0:T(8,128)(2,1)S(1)}, bf16[576,1536]{1,0:T(8,128)(2,1)}, u32[]{:S(2)}) copy-start(bf16[576,1536]{1,0:T(8,128)(2,1)} %param.25) | copy-start | bytes 5308420
  6.5 55.7 %copy-start.5 = (bf16[1536,128]{1,0:T(8,128)(2,1)S(1)}, bf16[1536,128]{1,0:T(8,128)(2,1)}, u32[]{:S(2)}) copy-start(bf16[1536,128]{1,0:T(8,128)(2,1)} %param.18) | copy-start | bytes 1179652
  6.5 343.3 %reduce-scatter.6.cloned.1.call-start = ((), (), s32[]{:S(2)}) async-start(), calls=%async_computation.2 | async-start | bytes 540672
  59.2 154.5 %copy-start.11 = (pred[72,128]{1,0:T(8,128)(4,1)}, pred[72,128]{1,0:T(8,128)(4,1)S(1)}, u32[]{:S(2)}) copy-start(pred[72,128]{1,0:T(8,128)(4,1)S(1)} %broadcast_compare_fusion) | copy-start | bytes 27652
  59.3 154.5 %copy-start.7 = (s32[72,128]{1,0:T(8,128)}, s32[72,128]{1,0:T(8,128)S(1)}, u32[]{:S(2)}) copy-start(s32[72,128]{1,0:T(8,128)S(1)} %iota_add_fusion) | copy-start | bytes 110596
  59.4 154.4 %copy-start.8 = (s32[72,4]{1,0:T(8,128)}, s32[72,4]{1,0:T(8,128)S(1)}, u32[]{:S(2)}) copy-start(s32[72,4]{1,0:T(8,128)S(1)} %add_add_fusion) | copy-start | bytes 3460
  88.8 125.0 %copy-start.10 = (f32[72,4,128]{2,1,0:T(4,128)}, f32[72,4,128]{2,1,0:T(4,128)S(1)}, u32[]{:S(2)}) copy-start(f32[72,4,128]{2,1,0:T(4,128)S(1)} %get-tuple-element.17) | copy-start | bytes 442372
  213.7 2.6 copy-start.9
  216.3 4.5 copy-start.6
  219.8 130.8 %copy-start.4 = (bf16[128,1536]{1,0:T(8,128)(2,1)S(1)}, bf16[128,1536]{1,0:T(8,128)(2,1)}, u32[]{:S(2)}) copy-start(bf16[128,1536]{1,0:T(8,128)(2,1)} %param.21) | copy-start | bytes 1179652
  220.7 206.7 %all-reduce.4.cloned.1.call-start = ((), (), s32[]{:S(2)}) async-start(), calls=%async_computation.1 | async-start | bytes 393216 | tf_op jit(solution)/shard_map/psum | solution.py:132
  349.8 82.1 %copy-start.12 = (f32[1536]{0:T(1024)S(1)}, f32[1536]{0:T(1024)}, u32[]{:S(2)}) copy-start(f32[1536]{0:T(1024)} %param.22) | copy-start | bytes 18436
  428.4 0.6 copy-start.2
  428.5 3.4 copy-start.1
  434.5 26.6 %copy-start.3 = (bf16[32,1536]{1,0:T(8,128)(2,1)S(1)}, bf16[32,1536]{1,0:T(8,128)(2,1)}, u32[]{:S(2)}) copy-start(bf16[32,1536]{1,0:T(8,128)(2,1)} %copy-done.2) | copy-start | bytes 294916
Sparse Core Ops, SparseCore 0:
  220.8 87.7 reduce-scatter.5
  351.7 75.6 all-reduce.3
